TPU v7x, 512 devices: a whole 4x8x8 slice. The times are simulated.
512 devices in a mesh: grp: 16 (over y, core), dev: 32 (over z, x).
Axes of the slice: x: 4, y: 8, z: 8, core: 2. Of those that a mesh axis runs over, the one named last changes fastest.
Arguments:
- panel_inverse: float32 [16, 32, 256, 256], P('grp', 'dev')
- coupling: float32 [16, 32, 256, 256], P('grp', 'dev'), may hold values from -0.875 to 0.875
- loads: float32 [16, 32, 16, 256], P('grp', 'dev'), may hold values from -6 to 6
- stiffness: float32 [24, 24], replicated
- element_substructure: int32 [16, 32, 1024], P('grp', 'dev'), may hold values from 0 to 31
- element_rows: int32 [16, 32, 24, 1024], P('grp', 'dev'), may hold values from 0 to 255
- element_density: float32 [16, 32, 1024], P('grp', 'dev'), may hold values from 0.2 to 1
- send_elements: int32 [16, 32, 32, 64], P('grp', 'dev'), may hold values from 0 to 1023
- receive_cells: int32 [16, 32, 32, 64], P('grp', 'dev'), may hold values from -1 to 16383, as said below
- design_density: float32 [16, 32, 128, 128], P('grp', 'dev'), may hold values from 0.3 to 1
- filter_offsets: int32 [8], replicated, may hold values from -3 to 3, as said below
- filter_weights: float32 [8], replicated, may hold values from 0.2 to 1
Outputs:
- interface: float32 [16, 32, 16, 256], P('grp', 'dev')
- filtered: float32 [16, 32, 128, 128], P('grp', 'dev')
Inputs may be any that keep to these rules, and one draw needn't show every extreme that they name: `receive_cells`: each receiver's slots from one source are filled in order: the first 64, 32, 16 or 8 hold a cell, the rest -1; in every group one owner is full from every source. `filter_offsets`: the offsets -3 and 3 are always among them; offsets may repeat.
All inputs are finite; a program needn't handle non-finite values.
Results may differ from a plain program's by a relative error of at most 0.0003.
Values sent between devices are 32-bit elements; how exact they have to be, the bound alone decides.
No kernel may reach another device: no remote copies, remote signals or barrier semaphores. Data moves between devices by JAX's collectives and lax.ppermute only.
A program may use at most 64 MiB of HBM per device.

v0:
```python
import jax
import jax.numpy as jnp
from jax import lax
from jax.sharding import PartitionSpec as P

NK = 8
RADIUS = 3
exact_mode = lax.Precision.HIGHEST
penalty = 3.0
energy_scale = 1.0 / 4096.0


def passed_along(value, axis, steps):
    count = lax.axis_size(axis)
    leading, last = (max(0, -steps), min(count, count - steps))
    return lax.ppermute(value, axis, [(source, source + steps) for source in range(leading, last)])


def padded_2(cells, sides, width):
    for axis, dim in sides:
        count = lax.axis_size(axis)
        ends = count - 1
        head = lax.slice_in_dim(cells, 0, width, axis=dim)
        tail = lax.slice_in_dim(cells, cells.shape[dim] - width, cells.shape[dim], axis=dim)
        cells = jnp.concatenate(
            [
                lax.ppermute(tail, axis, [(i, (i + 1) % count) for i in range(ends)]),
                cells,
                lax.ppermute(head, axis, [((i + 1) % count, i) for i in range(ends)]),
            ],
            axis=dim,
        )
    return cells


def product(left, right):
    return jnp.dot(left, right, precision=exact_mode, preferred_element_type=jnp.float32)


def on_device(
    panel_inverse,
    coupling,
    loads,
    stiffness,
    element_substructure,
    element_rows,
    element_density,
    send_elements,
    receive_cells,
    design_density,
    filter_offsets,
    filter_weights,
):
    inverse = panel_inverse[0, 0]
    couple = coupling[0, 0]
    rights = loads[0, 0]
    source = product(rights, inverse)

    def advance(level, current):
        previous = passed_along(current, "grp", 1)
        return product(rights - product(previous, couple), inverse)

    solved = lax.fori_loop(0, lax.axis_size("grp") - 1, advance, source)
    columns = lax.all_gather(solved, "dev", axis=1, tiled=True)
    panel_order = solved.shape[1]
    lookup = element_substructure[0, 0][None, :] * panel_order + element_rows[0, 0]
    motion = jnp.take(columns, lookup, axis=1)
    forces = jnp.einsum("ij,lje->lie", stiffness, motion, precision=exact_mode)
    energy = jnp.sum(motion * forces, axis=(0, 1))
    density = element_density[0, 0]
    sensitivity = -penalty * density * density * energy * energy_scale
    outgoing = jnp.take(sensitivity, send_elements[0, 0], axis=0)
    received = lax.all_to_all(outgoing, "dev", split_axis=0, concat_axis=0, tiled=True)
    owned = design_density[0, 0]
    row_count = owned.shape[0]
    cells = row_count * 128
    targets = receive_cells[0, 0]
    segment_ids = jnp.where(targets >= 0, targets, cells)
    collected = jax.ops.segment_sum(received.ravel(), segment_ids.ravel(), num_segments=cells + 1)[
        :cells
    ]
    weighted = owned * collected.reshape(row_count, 128)
    padded = padded_2(weighted, (("dev", 0),), RADIUS)
    total_rows = lax.axis_size("dev") * row_count
    global_rows = lax.axis_index("dev") * row_count + jnp.arange(row_count, dtype=jnp.int32)
    accum = jnp.zeros((row_count, 128), jnp.float32)
    weight_sum = jnp.zeros((row_count,), jnp.float32)
    for which in range(NK):
        offset = filter_offsets[which]
        window_rows = lax.dynamic_slice_in_dim(padded, RADIUS + offset, row_count, 0)
        inside = ((global_rows + offset >= 0) & (global_rows + offset < total_rows)).astype(
            jnp.float32
        )
        accum = accum + filter_weights[which] * window_rows
        weight_sum = weight_sum + filter_weights[which] * inside
    filtered = accum / (owned * weight_sum[:, None])
    return (solved[None, None], filtered[None, None])


def solution(mesh):
    placed = (
        P("grp", "dev", None, None),
        P("grp", "dev", None, None),
        P("grp", "dev", None, None),
        P(),
        P("grp", "dev", None),
        P("grp", "dev", None, None),
        P("grp", "dev", None),
        P("grp", "dev", None, None),
        P("grp", "dev", None, None),
        P("grp", "dev", None, None),
        P(),
        P(),
    )
    return jax.shard_map(
        on_device,
        mesh=mesh,
        in_specs=placed,
        out_specs=(P("grp", "dev", None, None), P("grp", "dev", None, None)),
        check_vma=False,
    )
```

profile of v0, /device:TPU:38, one launch (start us, length us, event | category | flops | bytes accessed | tf_op | source)
XLA Modules:
  0.0 357.8 jit_solution(10545197386665113381)
XLA Ops:
  4.4 129.7 %while.10 = (s32[]{:T(128)}, f32[16,256]{1,0:T(8,128)S(1)}, f32[256,256]{1,0:T(8,128)}, f32[16,256]{1,0:T(8,128)}, f32[256,256]{1,0:T(8,128)}, /*index=5*/s32[]{:T(128)}) while((s32[]{:T(128)}, f32[16,256]{1,0:T(8,128)S(1)}, f32[256,256]{1,0:T(8,128)}, f32[16,256]{1,0:T(8,128)}, f32[256,256]{1,0:T(8,128)}, /*index=5*/s32[]{:T(128)}) %tuple.42), condition=%wide.region_1.0_spmd, body=%wide.region_0.0_spmd.sunk | while | flops 25169920 | bytes 671853 | solution.py:63
  4.4 1.9 collective-permute-start
  6.3 4.3 %collective-permute-done = f32[16,256]{1,0:T(8,128)S(1)} collective-permute-done((f32[16,256]{1,0:T(8,128)S(1)}, f32[16,256]{1,0:T(8,128)S(1)}, u32[]{:S(2)}, u32[]{:S(2)}) %collective-permute-start) | collective-permute-done | bytes 16416 | tf_op jit(solution)/shard_map/while/body/eval_jaxpr/ppermute | solution.py:16
  10.7 1.2 convolution_subtract_fusion.2
  13.0 1.9 collective-permute-start
  15.0 4.3 %collective-permute-done = f32[16,256]{1,0:T(8,128)S(1)} collective-permute-done((f32[16,256]{1,0:T(8,128)S(1)}, f32[16,256]{1,0:T(8,128)S(1)}, u32[]{:S(2)}, u32[]{:S(2)}) %collective-permute-start) | collective-permute-done | bytes 16416 | tf_op jit(solution)/shard_map/while/body/eval_jaxpr/ppermute | solution.py:16
  19.3 1.2 convolution_subtract_fusion.2
  21.7 1.9 collective-permute-start
  23.6 4.3 %collective-permute-done = f32[16,256]{1,0:T(8,128)S(1)} collective-permute-done((f32[16,256]{1,0:T(8,128)S(1)}, f32[16,256]{1,0:T(8,128)S(1)}, u32[]{:S(2)}, u32[]{:S(2)}) %collective-permute-start) | collective-permute-done | bytes 16416 | tf_op jit(solution)/shard_map/while/body/eval_jaxpr/ppermute | solution.py:16
  27.9 1.2 convolution_subtract_fusion.2
  30.3 1.9 collective-permute-start
  32.3 4.3 %collective-permute-done = f32[16,256]{1,0:T(8,128)S(1)} collective-permute-done((f32[16,256]{1,0:T(8,128)S(1)}, f32[16,256]{1,0:T(8,128)S(1)}, u32[]{:S(2)}, u32[]{:S(2)}) %collective-permute-start) | collective-permute-done | bytes 16416 | tf_op jit(solution)/shard_map/while/body/eval_jaxpr/ppermute | solution.py:16
  36.6 1.2 convolution_subtract_fusion.2
  39.0 1.9 collective-permute-start
  40.9 4.3 %collective-permute-done = f32[16,256]{1,0:T(8,128)S(1)} collective-permute-done((f32[16,256]{1,0:T(8,128)S(1)}, f32[16,256]{1,0:T(8,128)S(1)}, u32[]{:S(2)}, u32[]{:S(2)}) %collective-permute-start) | collective-permute-done | bytes 16416 | tf_op jit(solution)/shard_map/while/body/eval_jaxpr/ppermute | solution.py:16
  45.2 1.2 convolution_subtract_fusion.2
  47.6 1.9 collective-permute-start
  49.5 4.3 %collective-permute-done = f32[16,256]{1,0:T(8,128)S(1)} collective-permute-done((f32[16,256]{1,0:T(8,128)S(1)}, f32[16,256]{1,0:T(8,128)S(1)}, u32[]{:S(2)}, u32[]{:S(2)}) %collective-permute-start) | collective-permute-done | bytes 16416 | tf_op jit(solution)/shard_map/while/body/eval_jaxpr/ppermute | solution.py:16
  53.9 1.2 convolution_subtract_fusion.2
  56.3 1.9 collective-permute-start
  58.2 4.3 %collective-permute-done = f32[16,256]{1,0:T(8,128)S(1)} collective-permute-done((f32[16,256]{1,0:T(8,128)S(1)}, f32[16,256]{1,0:T(8,128)S(1)}, u32[]{:S(2)}, u32[]{:S(2)}) %collective-permute-start) | collective-permute-done | bytes 16416 | tf_op jit(solution)/shard_map/while/body/eval_jaxpr/ppermute | solution.py:16
  64.9 1.9 collective-permute-start
  66.8 4.3 %collective-permute-done = f32[16,256]{1,0:T(8,128)S(1)} collective-permute-done((f32[16,256]{1,0:T(8,128)S(1)}, f32[16,256]{1,0:T(8,128)S(1)}, u32[]{:S(2)}, u32[]{:S(2)}) %collective-permute-start) | collective-permute-done | bytes 16416 | tf_op jit(solution)/shard_map/while/body/eval_jaxpr/ppermute | solution.py:16
  73.6 1.9 collective-permute-start
  75.5 4.3 %collective-permute-done = f32[16,256]{1,0:T(8,128)S(1)} collective-permute-done((f32[16,256]{1,0:T(8,128)S(1)}, f32[16,256]{1,0:T(8,128)S(1)}, u32[]{:S(2)}, u32[]{:S(2)}) %collective-permute-start) | collective-permute-done | bytes 16416 | tf_op jit(solution)/shard_map/while/body/eval_jaxpr/ppermute | solution.py:16
  82.2 1.9 collective-permute-start
  84.1 4.3 %collective-permute-done = f32[16,256]{1,0:T(8,128)S(1)} collective-permute-done((f32[16,256]{1,0:T(8,128)S(1)}, f32[16,256]{1,0:T(8,128)S(1)}, u32[]{:S(2)}, u32[]{:S(2)}) %collective-permute-start) | collective-permute-done | bytes 16416 | tf_op jit(solution)/shard_map/while/body/eval_jaxpr/ppermute | solution.py:16
  90.9 1.9 collective-permute-start
  92.8 4.3 %collective-permute-done = f32[16,256]{1,0:T(8,128)S(1)} collective-permute-done((f32[16,256]{1,0:T(8,128)S(1)}, f32[16,256]{1,0:T(8,128)S(1)}, u32[]{:S(2)}, u32[]{:S(2)}) %collective-permute-start) | collective-permute-done | bytes 16416 | tf_op jit(solution)/shard_map/while/body/eval_jaxpr/ppermute | solution.py:16
  99.5 1.9 collective-permute-start
  101.4 4.3 %collective-permute-done = f32[16,256]{1,0:T(8,128)S(1)} collective-permute-done((f32[16,256]{1,0:T(8,128)S(1)}, f32[16,256]{1,0:T(8,128)S(1)}, u32[]{:S(2)}, u32[]{:S(2)}) %collective-permute-start) | collective-permute-done | bytes 16416 | tf_op jit(solution)/shard_map/while/body/eval_jaxpr/ppermute | solution.py:16
  108.2 1.9 collective-permute-start
  110.1 4.3 %collective-permute-done = f32[16,256]{1,0:T(8,128)S(1)} collective-permute-done((f32[16,256]{1,0:T(8,128)S(1)}, f32[16,256]{1,0:T(8,128)S(1)}, u32[]{:S(2)}, u32[]{:S(2)}) %collective-permute-start) | collective-permute-done | bytes 16416 | tf_op jit(solution)/shard_map/while/body/eval_jaxpr/ppermute | solution.py:16
  116.8 1.9 collective-permute-start
  118.7 4.3 %collective-permute-done = f32[16,256]{1,0:T(8,128)S(1)} collective-permute-done((f32[16,256]{1,0:T(8,128)S(1)}, f32[16,256]{1,0:T(8,128)S(1)}, u32[]{:S(2)}, u32[]{:S(2)}) %collective-permute-start) | collective-permute-done | bytes 16416 | tf_op jit(solution)/shard_map/while/body/eval_jaxpr/ppermute | solution.py:16
  125.4 1.9 collective-permute-start
  127.4 4.3 %collective-permute-done = f32[16,256]{1,0:T(8,128)S(1)} collective-permute-done((f32[16,256]{1,0:T(8,128)S(1)}, f32[16,256]{1,0:T(8,128)S(1)}, u32[]{:S(2)}, u32[]{:S(2)}) %collective-permute-start) | collective-permute-done | bytes 16416 | tf_op jit(solution)/shard_map/while/body/eval_jaxpr/ppermute | solution.py:16
  134.2 64.9 %all_gather.3 = f32[16,8192]{0,1:T(8,128)} all-gather(f32[16,256]{0,1:T(8,128)S(1)} %copy.18), channel_id=1, replica_groups=mesh['grp'=16,'dev'=32] {'dev'}, dimensions={1}, use_global_device_ids=true | all-gather | bytes 540672 | tf_op jit(solution)/shard_map/all_gather | solution.py:64
  199.2 84.1 %gather_fusion = f32[24576,16]{1,0:T(8,128)} fusion(f32[16,8192]{0,1:T(8,128)} %all_gather.3, s32[24576]{0:T(1024)S(1)} %broadcast_clamp_fusion), kind=kCustom, calls=%fused_computation | custom fusion | bytes 3244032 | tf_op jit(solution)/shard_map/jit(_take)/gather | solution.py:67
  283.3 7.7 %copy.20 = f32[24,1024,16]{1,0,2:T(8,128)S(1)} copy(f32[24,1024,16]{2,1,0:T(8,128)} %bitcast.87) | data formatting | bytes 3145728 | tf_op jit(solution)/shard_map/jit(_take)/gather | solution.py:67
  291.1 1.7 fusion
  292.8 8.6 %gather_fusion.1 = f32[2048]{0:T(1024)S(1)} fusion(f32[1024]{0:T(1024)S(1)} %fusion.16, s32[2048]{0:T(1024)S(1)} %broadcast_clamp_fusion.1), kind=kCustom, calls=%fused_computation.1 | custom fusion | bytes 24576 | tf_op jit(solution)/shard_map/jit(_take)/gather | solution.py:72
  302.1 6.3 %all-to-all-start = ((f32[32,1,64]{2,1,0:T(1,128)}), f32[32,1,64]{2,1,0:T(1,128)S(1)}, u32[]{:S(2)}, u32[]{:S(2)}) async-start(f32[32,1,64]{2,1,0:T(1,128)} %and_select_fusion), calls=%async_computation | async-start | bytes 32768 | tf_op jit(solution)/shard_map/all_to_all | solution.py:73
  309.9 10.0 %fusion.23 = f32[128]{0:T(128)S(1)} fusion(f32[]{:T(128)} %bitcast.31, s32[]{:T(128)} %bitcast.32, f32[]{:T(128)} %bitcast.29, s32[]{:T(128)} %bitcast.30, f32[]{:T(128)} %bitcast.27, s32[]{:T(128)} %bitcast.28, f32[]{:T(128)} %bitcast.25, s32[]{:T(128)} %bitcast.26, f32[]{:T(128)} %bitcast.23, s32[]{:T(128)} %bitcast.24, f32[]{:T(128)} %bitcast.21, ...), kind=kLoop, calls=%fused_computation.50 | loop fusion | flops 6144 | bytes 580 | tf_op jit(solution)/shard_map/add | solution.py:95
  322.5 12.7 %scatter_custom_fusion = f32[16385]{0:T(1024)S(1)} fusion(s32[2048]{0:T(1024)S(1)} %bitcast.96, f32[2048]{0:T(1024)S(1)} %reshape.242, f32[]{:T(128)} %constant.61.clone.1), kind=kCustom, calls=%fused_computation.28 | custom fusion | flops 2048 | bytes 65544 | tf_op jit(solution)/shard_map/scatter-add | solution.py:79
  335.3 2.9 collective-permute-start.2
  338.2 5.0 %collective-permute-start.1 = (f32[3,128]{1,0:T(4,128)S(1)}, f32[3,128]{1,0:T(4,128)S(1)}, u32[]{:S(2)}, u32[]{:S(2)}) collective-permute-start(f32[3,128]{1,0:T(4,128)S(1)} %get-tuple-element.40), channel_id=1, source_target_pairs={{0,1},{1,2},{2,3},{3,4},{4,5},{5,6},{6,7},{7,8},{8,9},{9,10},{10,1... | collective-permute-start | bytes 4616 | tf_op jit(solution)/shard_map/ppermute | solution.py:27
  352.1 5.7 %fusion.11 = f32[1,1,128,128]{3,2,1,0:T(8,128)} fusion(f32[1,1,128,128]{3,2,1,0:T(8,128)S(1)} %copy-done.1, f32[134,128]{1,0:T(8,128)S(1)} %pad_maximum_fusion, s32[]{:T(128)S(6)} %select_n.103, s32[]{:T(128)S(6)} %select_n.102, s32[]{:T(128)S(6)} %select_n.101, s32[]{:T(128)S(6)} %select_n.100, s32[]{:T(128)S(6)} %select_n.99, s32[]{:T(128)S(6)} %select_n.98, ...), kind=kLoop, calls=%fused_computation.23 | loop fusion | flops 278528 | bytes 655936 | tf_op jit(solution)/shard_map/broadcast_in_dim | solution.py:97
  (66 shorter events, 35.3 us)
Async XLA Ops:
  0.6 290.4 %copy-start = (f32[24,24]{1,0:T(8,128)S(1)}, f32[24,24]{1,0:T(8,128)}, u32[]{:S(2)}) copy-start(f32[24,24]{1,0:T(8,128)} %param.17) | copy-start | bytes 6916
  4.4 6.3 %collective-permute-start = (f32[16,256]{1,0:T(8,128)S(1)}, f32[16,256]{1,0:T(8,128)S(1)}, u32[]{:S(2)}, u32[]{:S(2)}) collective-permute-start(f32[16,256]{1,0:T(8,128)S(1)} %get-tuple-element.96), channel_id=1, source_target_pairs={{0,32},{32,64},{64,96},{96,128},{128,160},{160,192},{192,224},{224... | collective-permute-start | bytes 49160 | tf_op jit(solution)/shard_map/while/body/eval_jaxpr/ppermute | solution.py:16
  13.0 6.3 %collective-permute-start = (f32[16,256]{1,0:T(8,128)S(1)}, f32[16,256]{1,0:T(8,128)S(1)}, u32[]{:S(2)}, u32[]{:S(2)}) collective-permute-start(f32[16,256]{1,0:T(8,128)S(1)} %get-tuple-element.96), channel_id=1, source_target_pairs={{0,32},{32,64},{64,96},{96,128},{128,160},{160,192},{192,224},{224... | collective-permute-start | bytes 49160 | tf_op jit(solution)/shard_map/while/body/eval_jaxpr/ppermute | solution.py:16
  21.7 6.3 %collective-permute-start = (f32[16,256]{1,0:T(8,128)S(1)}, f32[16,256]{1,0:T(8,128)S(1)}, u32[]{:S(2)}, u32[]{:S(2)}) collective-permute-start(f32[16,256]{1,0:T(8,128)S(1)} %get-tuple-element.96), channel_id=1, source_target_pairs={{0,32},{32,64},{64,96},{96,128},{128,160},{160,192},{192,224},{224... | collective-permute-start | bytes 49160 | tf_op jit(solution)/shard_map/while/body/eval_jaxpr/ppermute | solution.py:16
  30.3 6.3 %collective-permute-start = (f32[16,256]{1,0:T(8,128)S(1)}, f32[16,256]{1,0:T(8,128)S(1)}, u32[]{:S(2)}, u32[]{:S(2)}) collective-permute-start(f32[16,256]{1,0:T(8,128)S(1)} %get-tuple-element.96), channel_id=1, source_target_pairs={{0,32},{32,64},{64,96},{96,128},{128,160},{160,192},{192,224},{224... | collective-permute-start | bytes 49160 | tf_op jit(solution)/shard_map/while/body/eval_jaxpr/ppermute | solution.py:16
  39.0 6.3 %collective-permute-start = (f32[16,256]{1,0:T(8,128)S(1)}, f32[16,256]{1,0:T(8,128)S(1)}, u32[]{:S(2)}, u32[]{:S(2)}) collective-permute-start(f32[16,256]{1,0:T(8,128)S(1)} %get-tuple-element.96), channel_id=1, source_target_pairs={{0,32},{32,64},{64,96},{96,128},{128,160},{160,192},{192,224},{224... | collective-permute-start | bytes 49160 | tf_op jit(solution)/shard_map/while/body/eval_jaxpr/ppermute | solution.py:16
  47.6 6.3 %collective-permute-start = (f32[16,256]{1,0:T(8,128)S(1)}, f32[16,256]{1,0:T(8,128)S(1)}, u32[]{:S(2)}, u32[]{:S(2)}) collective-permute-start(f32[16,256]{1,0:T(8,128)S(1)} %get-tuple-element.96), channel_id=1, source_target_pairs={{0,32},{32,64},{64,96},{96,128},{128,160},{160,192},{192,224},{224... | collective-permute-start | bytes 49160 | tf_op jit(solution)/shard_map/while/body/eval_jaxpr/ppermute | solution.py:16
  56.3 6.3 %collective-permute-start = (f32[16,256]{1,0:T(8,128)S(1)}, f32[16,256]{1,0:T(8,128)S(1)}, u32[]{:S(2)}, u32[]{:S(2)}) collective-permute-start(f32[16,256]{1,0:T(8,128)S(1)} %get-tuple-element.96), channel_id=1, source_target_pairs={{0,32},{32,64},{64,96},{96,128},{128,160},{160,192},{192,224},{224... | collective-permute-start | bytes 49160 | tf_op jit(solution)/shard_map/while/body/eval_jaxpr/ppermute | solution.py:16
  64.9 6.3 %collective-permute-start = (f32[16,256]{1,0:T(8,128)S(1)}, f32[16,256]{1,0:T(8,128)S(1)}, u32[]{:S(2)}, u32[]{:S(2)}) collective-permute-start(f32[16,256]{1,0:T(8,128)S(1)} %get-tuple-element.96), channel_id=1, source_target_pairs={{0,32},{32,64},{64,96},{96,128},{128,160},{160,192},{192,224},{224... | collective-permute-start | bytes 49160 | tf_op jit(solution)/shard_map/while/body/eval_jaxpr/ppermute | solution.py:16
  73.6 6.3 %collective-permute-start = (f32[16,256]{1,0:T(8,128)S(1)}, f32[16,256]{1,0:T(8,128)S(1)}, u32[]{:S(2)}, u32[]{:S(2)}) collective-permute-start(f32[16,256]{1,0:T(8,128)S(1)} %get-tuple-element.96), channel_id=1, source_target_pairs={{0,32},{32,64},{64,96},{96,128},{128,160},{160,192},{192,224},{224... | collective-permute-start | bytes 49160 | tf_op jit(solution)/shard_map/while/body/eval_jaxpr/ppermute | solution.py:16
  82.2 6.3 %collective-permute-start = (f32[16,256]{1,0:T(8,128)S(1)}, f32[16,256]{1,0:T(8,128)S(1)}, u32[]{:S(2)}, u32[]{:S(2)}) collective-permute-start(f32[16,256]{1,0:T(8,128)S(1)} %get-tuple-element.96), channel_id=1, source_target_pairs={{0,32},{32,64},{64,96},{96,128},{128,160},{160,192},{192,224},{224... | collective-permute-start | bytes 49160 | tf_op jit(solution)/shard_map/while/body/eval_jaxpr/ppermute | solution.py:16
  90.9 6.3 %collective-permute-start = (f32[16,256]{1,0:T(8,128)S(1)}, f32[16,256]{1,0:T(8,128)S(1)}, u32[]{:S(2)}, u32[]{:S(2)}) collective-permute-start(f32[16,256]{1,0:T(8,128)S(1)} %get-tuple-element.96), channel_id=1, source_target_pairs={{0,32},{32,64},{64,96},{96,128},{128,160},{160,192},{192,224},{224... | collective-permute-start | bytes 49160 | tf_op jit(solution)/shard_map/while/body/eval_jaxpr/ppermute | solution.py:16
  99.5 6.3 %collective-permute-start = (f32[16,256]{1,0:T(8,128)S(1)}, f32[16,256]{1,0:T(8,128)S(1)}, u32[]{:S(2)}, u32[]{:S(2)}) collective-permute-start(f32[16,256]{1,0:T(8,128)S(1)} %get-tuple-element.96), channel_id=1, source_target_pairs={{0,32},{32,64},{64,96},{96,128},{128,160},{160,192},{192,224},{224... | collective-permute-start | bytes 49160 | tf_op jit(solution)/shard_map/while/body/eval_jaxpr/ppermute | solution.py:16
  108.2 6.3 %collective-permute-start = (f32[16,256]{1,0:T(8,128)S(1)}, f32[16,256]{1,0:T(8,128)S(1)}, u32[]{:S(2)}, u32[]{:S(2)}) collective-permute-start(f32[16,256]{1,0:T(8,128)S(1)} %get-tuple-element.96), channel_id=1, source_target_pairs={{0,32},{32,64},{64,96},{96,128},{128,160},{160,192},{192,224},{224... | collective-permute-start | bytes 49160 | tf_op jit(solution)/shard_map/while/body/eval_jaxpr/ppermute | solution.py:16
  116.8 6.3 %collective-permute-start = (f32[16,256]{1,0:T(8,128)S(1)}, f32[16,256]{1,0:T(8,128)S(1)}, u32[]{:S(2)}, u32[]{:S(2)}) collective-permute-start(f32[16,256]{1,0:T(8,128)S(1)} %get-tuple-element.96), channel_id=1, source_target_pairs={{0,32},{32,64},{64,96},{96,128},{128,160},{160,192},{192,224},{224... | collective-permute-start | bytes 49160 | tf_op jit(solution)/shard_map/while/body/eval_jaxpr/ppermute | solution.py:16
  125.4 6.3 %collective-permute-start = (f32[16,256]{1,0:T(8,128)S(1)}, f32[16,256]{1,0:T(8,128)S(1)}, u32[]{:S(2)}, u32[]{:S(2)}) collective-permute-start(f32[16,256]{1,0:T(8,128)S(1)} %get-tuple-element.96), channel_id=1, source_target_pairs={{0,32},{32,64},{64,96},{96,128},{128,160},{160,192},{192,224},{224... | collective-permute-start | bytes 49160 | tf_op jit(solution)/shard_map/while/body/eval_jaxpr/ppermute | solution.py:16
  134.1 65.0 %copy-start.2 = (f32[16,256]{1,0:T(8,128)}, f32[16,256]{1,0:T(8,128)S(1)}, u32[]{:S(2)}) copy-start(f32[16,256]{1,0:T(8,128)S(1)} %get-tuple-element.29) | copy-start | bytes 49156
  283.3 7.7 %copy-start.3 = (s32[1,1,32,64]{3,2,1,0:T(8,128)S(1)}, s32[1,1,32,64]{3,2,1,0:T(8,128)}, u32[]{:S(2)}) copy-start(s32[1,1,32,64]{3,2,1,0:T(8,128)} %param.21) | copy-start | bytes 24580
  290.9 1.8 copy-start.7
  292.8 15.7 %copy-start.6 = (s32[1,1,32,64]{3,2,1,0:T(8,128)S(1)}, s32[1,1,32,64]{3,2,1,0:T(8,128)}, u32[]{:S(2)}) copy-start(s32[1,1,32,64]{3,2,1,0:T(8,128)} %param.22) | copy-start | bytes 24580
  292.8 15.8 %copy-start.4 = (s32[8]{0:T(128)S(1)}, s32[8]{0:T(128)}, u32[]{:S(2)}) copy-start(s32[8]{0:T(128)} %param.24) | copy-start | bytes 100
  292.8 16.5 %copy-start.5 = (f32[8]{0:T(128)S(1)}, f32[8]{0:T(128)}, u32[]{:S(2)}) copy-start(f32[8]{0:T(128)} %param.25) | copy-start | bytes 100
  292.8 42.4 %copy-start.1 = (f32[1,1,128,128]{3,2,1,0:T(8,128)S(1)}, f32[1,1,128,128]{3,2,1,0:T(8,128)}, u32[]{:S(2)}) copy-start(f32[1,1,128,128]{3,2,1,0:T(8,128)} %param.23) | copy-start | bytes 196612
  302.1 19.0 %all-to-all-start = ((f32[32,1,64]{2,1,0:T(1,128)}), f32[32,1,64]{2,1,0:T(1,128)S(1)}, u32[]{:S(2)}, u32[]{:S(2)}) async-start(f32[32,1,64]{2,1,0:T(1,128)} %and_select_fusion), calls=%async_computation | async-start | bytes 32768 | tf_op jit(solution)/shard_map/all_to_all | solution.py:73
  335.3 16.8 %collective-permute-start.2 = (f32[3,128]{1,0:T(4,128)S(1)}, f32[3,128]{1,0:T(4,128)S(1)}, u32[]{:S(2)}, u32[]{:S(2)}) collective-permute-start(f32[3,128]{1,0:T(4,128)S(1)} %get-tuple-element.41), channel_id=1, source_target_pairs={{1,0},{2,1},{3,2},{4,3},{5,4},{6,5},{7,6},{8,7},{9,8},{10,9},{11,1... | collective-permute-start | bytes 4616 | tf_op jit(solution)/shard_map/ppermute | solution.py:29
  338.2 13.8 %collective-permute-start.1 = (f32[3,128]{1,0:T(4,128)S(1)}, f32[3,128]{1,0:T(4,128)S(1)}, u32[]{:S(2)}, u32[]{:S(2)}) collective-permute-start(f32[3,128]{1,0:T(4,128)S(1)} %get-tuple-element.40), channel_id=1, source_target_pairs={{0,1},{1,2},{2,3},{3,4},{4,5},{5,6},{6,7},{7,8},{8,9},{9,10},{10,1... | collective-permute-start | bytes 4616 | tf_op jit(solution)/shard_map/ppermute | solution.py:27
where the time goes:
time: 360 us; the launch traced here: 358 us
  local copies, waits for them, and re-layouts  103 us (29%)
  waiting for transfers between devices  65.1 us (18%)
  blocking collectives  64.9 us (18%)
  starting transfers between devices  43.1 us (12%)
  matrix products  37.8 us (10%)
  other arithmetic  32.4 us (9%)
  between operations  10.9 us (3%)
    gather x2, local copies, waits for them, and re-layouts, on_device(): motion = jnp.take(columns, lookup, axis=1)  91.8 us
    ppermute x15, waiting for transfers between devices, passed_along(): lax.ppermute(value, axis, [(source, source + steps) for source in range(l...  65.1 us
    all_gather x1, blocking collectives, on_device(): columns = lax.all_gather(solved, 'dev', axis=1, tiled=True)  64.9 us
    dot_general x31, matrix products, product(): jnp.dot(left, right, precision=exact_mode, preferred_element_type=jnp.flo...  36.1 us
    ppermute x15, starting transfers between devices, passed_along(): lax.ppermute(value, axis, [(source, source + steps) for source in range(l...  28.8 us
    scatter-add x1, other arithmetic, on_device(): jax.ops.segment_sum(received.ravel(), segment_ids.ravel(), num_segments=c...  12.7 us
    add x1, other arithmetic, on_device(): weight_sum = weight_sum + filter_weights[which] * inside  10 us
    gather x2, local copies, waits for them, and re-layouts, on_device(): outgoing = jnp.take(sensitivity, send_elements[0, 0], axis=0)  8.67 us
  transfers between devices with their start and end apart: 18, of which 15 were waited for; matrix products, arithmetic and copies ran while one was open for 3% of the time, Pallas kernels for 0%

commit v1 on v0

--- a/solution.py
+++ b/solution.py
@@ -61,7 +61,9 @@
         return product(rights - product(previous, couple), inverse)
 
     solved = lax.fori_loop(0, lax.axis_size("grp") - 1, advance, source)
-    columns = lax.all_gather(solved, "dev", axis=1, tiled=True)
+    columns = jnp.concatenate(
+        lax.all_to_all(jnp.stack([solved] * lax.axis_size("dev")), "dev", 0, 0), axis=1
+    )
     panel_order = solved.shape[1]
     lookup = element_substructure[0, 0][None, :] * panel_order + element_rows[0, 0]
     motion = jnp.take(columns, lookup, axis=1)

time: 360 us -> 320 us (0.89)
  blocking collectives: 64.9 us -> 0 us
  starting transfers between devices: 43.1 us -> 55.7 us
  waiting for transfers between devices: 65.1 us -> 77.2 us
    all_gather x1 -> x0, blocking collectives: 64.9 us -> none  [on_device(): columns = lax.all_gather(solved, 'dev', axis=1, tiled=True)]
    all_to_all x0 -> x1, starting transfers between devices: none -> 13.4 us  [on_device(): lax.all_to_all(jnp.stack([solved] * lax.axis_size('dev')), 'dev', 0, 0)]
    all_to_all x0 -> x1, waiting for transfers between devices: none -> 12.1 us  [on_device(): lax.all_to_all(jnp.stack([solved] * lax.axis_size('dev')), 'dev', 0, 0)]
  transfers between devices with their start and end apart: 18 -> 19, of which waited for: 15 -> 16; matrix products, arithmetic and copies ran while one was open for 3% -> 4% of each run, Pallas kernels for 0% -> 0%
where the time goes in v1:
time: 320 us; the launch traced here: 318 us
  local copies, waits for them, and re-layouts  106 us (33%)
  waiting for transfers between devices  77.2 us (24%)
  starting transfers between devices  55.7 us (17%)
  matrix products  37.8 us (12%)
  other arithmetic  30.1 us (9%)
  between operations  10.7 us (3%)
    gather x2, local copies, waits for them, and re-layouts, on_device(): motion = jnp.take(columns, lookup, axis=1)  91.7 us
    ppermute x15, waiting for transfers between devices, passed_along(): lax.ppermute(value, axis, [(source, source + steps) for source in range(l...  65.1 us
    dot_general x31, matrix products, product(): jnp.dot(left, right, precision=exact_mode, preferred_element_type=jnp.flo...  36.1 us
    ppermute x15, starting transfers between devices, passed_along(): lax.ppermute(value, axis, [(source, source + steps) for source in range(l...  28.8 us
    all_to_all x1, starting transfers between devices, on_device(): lax.all_to_all(jnp.stack([solved] * lax.axis_size('dev')), 'dev', 0, 0)  13.4 us
    scatter-add x1, other arithmetic, on_device(): jax.ops.segment_sum(received.ravel(), segment_ids.ravel(), num_segments=c...  12.7 us
    all_to_all x1, waiting for transfers between devices, on_device(): lax.all_to_all(jnp.stack([solved] * lax.axis_size('dev')), 'dev', 0, 0)  12.1 us
    add x1, other arithmetic, on_device(): weight_sum = weight_sum + filter_weights[which] * inside  10 us
  transfers between devices with their start and end apart: 19, of which 16 were waited for; matrix products, arithmetic and copies ran while one was open for 4% of the time, Pallas kernels for 0%

profile of v1, /device:TPU:38, one launch (start us, length us, event | category | flops | bytes accessed | tf_op | source)
XLA Modules:
  0.0 318.4 jit_solution(12566488111940631395)
XLA Ops:
  1.8 129.7 %while.10 = (s32[]{:T(128)}, f32[16,256]{1,0:T(8,128)S(1)}, f32[256,256]{1,0:T(8,128)}, f32[16,256]{1,0:T(8,128)}, f32[256,256]{1,0:T(8,128)}, /*index=5*/s32[]{:T(128)}) while((s32[]{:T(128)}, f32[16,256]{1,0:T(8,128)S(1)}, f32[256,256]{1,0:T(8,128)}, f32[16,256]{1,0:T(8,128)}, f32[256,256]{1,0:T(8,128)}, /*index=5*/s32[]{:T(128)}) %tuple.42), condition=%wide.region_1.0_spmd, body=%wide.region_0.0_spmd.sunk | while | flops 25169920 | bytes 671853 | solution.py:63
  1.8 1.9 collective-permute-start
  3.8 4.3 %collective-permute-done = f32[16,256]{1,0:T(8,128)S(1)} collective-permute-done((f32[16,256]{1,0:T(8,128)S(1)}, f32[16,256]{1,0:T(8,128)S(1)}, u32[]{:S(2)}, u32[]{:S(2)}) %collective-permute-start) | collective-permute-done | bytes 16416 | tf_op jit(solution)/shard_map/while/body/eval_jaxpr/ppermute | solution.py:16
  8.1 1.2 convolution_subtract_fusion.2
  10.5 1.9 collective-permute-start
  12.4 4.3 %collective-permute-done = f32[16,256]{1,0:T(8,128)S(1)} collective-permute-done((f32[16,256]{1,0:T(8,128)S(1)}, f32[16,256]{1,0:T(8,128)S(1)}, u32[]{:S(2)}, u32[]{:S(2)}) %collective-permute-start) | collective-permute-done | bytes 16416 | tf_op jit(solution)/shard_map/while/body/eval_jaxpr/ppermute | solution.py:16
  16.8 1.2 convolution_subtract_fusion.2
  19.1 1.9 collective-permute-start
  21.1 4.3 %collective-permute-done = f32[16,256]{1,0:T(8,128)S(1)} collective-permute-done((f32[16,256]{1,0:T(8,128)S(1)}, f32[16,256]{1,0:T(8,128)S(1)}, u32[]{:S(2)}, u32[]{:S(2)}) %collective-permute-start) | collective-permute-done | bytes 16416 | tf_op jit(solution)/shard_map/while/body/eval_jaxpr/ppermute | solution.py:16
  25.4 1.2 convolution_subtract_fusion.2
  27.8 1.9 collective-permute-start
  29.7 4.3 %collective-permute-done = f32[16,256]{1,0:T(8,128)S(1)} collective-permute-done((f32[16,256]{1,0:T(8,128)S(1)}, f32[16,256]{1,0:T(8,128)S(1)}, u32[]{:S(2)}, u32[]{:S(2)}) %collective-permute-start) | collective-permute-done | bytes 16416 | tf_op jit(solution)/shard_map/while/body/eval_jaxpr/ppermute | solution.py:16
  34.1 1.2 convolution_subtract_fusion.2
  36.4 1.9 collective-permute-start
  38.4 4.3 %collective-permute-done = f32[16,256]{1,0:T(8,128)S(1)} collective-permute-done((f32[16,256]{1,0:T(8,128)S(1)}, f32[16,256]{1,0:T(8,128)S(1)}, u32[]{:S(2)}, u32[]{:S(2)}) %collective-permute-start) | collective-permute-done | bytes 16416 | tf_op jit(solution)/shard_map/while/body/eval_jaxpr/ppermute | solution.py:16
  45.1 1.9 collective-permute-start
  47.0 4.3 %collective-permute-done = f32[16,256]{1,0:T(8,128)S(1)} collective-permute-done((f32[16,256]{1,0:T(8,128)S(1)}, f32[16,256]{1,0:T(8,128)S(1)}, u32[]{:S(2)}, u32[]{:S(2)}) %collective-permute-start) | collective-permute-done | bytes 16416 | tf_op jit(solution)/shard_map/while/body/eval_jaxpr/ppermute | solution.py:16
  53.7 1.9 collective-permute-start
  55.7 4.3 %collective-permute-done = f32[16,256]{1,0:T(8,128)S(1)} collective-permute-done((f32[16,256]{1,0:T(8,128)S(1)}, f32[16,256]{1,0:T(8,128)S(1)}, u32[]{:S(2)}, u32[]{:S(2)}) %collective-permute-start) | collective-permute-done | bytes 16416 | tf_op jit(solution)/shard_map/while/body/eval_jaxpr/ppermute | solution.py:16
  62.4 1.9 collective-permute-start
  64.3 4.3 %collective-permute-done = f32[16,256]{1,0:T(8,128)S(1)} collective-permute-done((f32[16,256]{1,0:T(8,128)S(1)}, f32[16,256]{1,0:T(8,128)S(1)}, u32[]{:S(2)}, u32[]{:S(2)}) %collective-permute-start) | collective-permute-done | bytes 16416 | tf_op jit(solution)/shard_map/while/body/eval_jaxpr/ppermute | solution.py:16
  71.0 1.9 collective-permute-start
  73.0 4.3 %collective-permute-done = f32[16,256]{1,0:T(8,128)S(1)} collective-permute-done((f32[16,256]{1,0:T(8,128)S(1)}, f32[16,256]{1,0:T(8,128)S(1)}, u32[]{:S(2)}, u32[]{:S(2)}) %collective-permute-start) | collective-permute-done | bytes 16416 | tf_op jit(solution)/shard_map/while/body/eval_jaxpr/ppermute | solution.py:16
  79.7 1.9 collective-permute-start
  81.6 4.3 %collective-permute-done = f32[16,256]{1,0:T(8,128)S(1)} collective-permute-done((f32[16,256]{1,0:T(8,128)S(1)}, f32[16,256]{1,0:T(8,128)S(1)}, u32[]{:S(2)}, u32[]{:S(2)}) %collective-permute-start) | collective-permute-done | bytes 16416 | tf_op jit(solution)/shard_map/while/body/eval_jaxpr/ppermute | solution.py:16
  88.3 1.9 collective-permute-start
  90.2 4.3 %collective-permute-done = f32[16,256]{1,0:T(8,128)S(1)} collective-permute-done((f32[16,256]{1,0:T(8,128)S(1)}, f32[16,256]{1,0:T(8,128)S(1)}, u32[]{:S(2)}, u32[]{:S(2)}) %collective-permute-start) | collective-permute-done | bytes 16416 | tf_op jit(solution)/shard_map/while/body/eval_jaxpr/ppermute | solution.py:16
  97.0 1.9 collective-permute-start
  98.9 4.3 %collective-permute-done = f32[16,256]{1,0:T(8,128)S(1)} collective-permute-done((f32[16,256]{1,0:T(8,128)S(1)}, f32[16,256]{1,0:T(8,128)S(1)}, u32[]{:S(2)}, u32[]{:S(2)}) %collective-permute-start) | collective-permute-done | bytes 16416 | tf_op jit(solution)/shard_map/while/body/eval_jaxpr/ppermute | solution.py:16
  105.6 1.9 collective-permute-start
  107.5 4.3 %collective-permute-done = f32[16,256]{1,0:T(8,128)S(1)} collective-permute-done((f32[16,256]{1,0:T(8,128)S(1)}, f32[16,256]{1,0:T(8,128)S(1)}, u32[]{:S(2)}, u32[]{:S(2)}) %collective-permute-start) | collective-permute-done | bytes 16416 | tf_op jit(solution)/shard_map/while/body/eval_jaxpr/ppermute | solution.py:16
  114.3 1.9 collective-permute-start
  116.2 4.3 %collective-permute-done = f32[16,256]{1,0:T(8,128)S(1)} collective-permute-done((f32[16,256]{1,0:T(8,128)S(1)}, f32[16,256]{1,0:T(8,128)S(1)}, u32[]{:S(2)}, u32[]{:S(2)}) %collective-permute-start) | collective-permute-done | bytes 16416 | tf_op jit(solution)/shard_map/while/body/eval_jaxpr/ppermute | solution.py:16
  122.9 1.9 collective-permute-start
  124.8 4.3 %collective-permute-done = f32[16,256]{1,0:T(8,128)S(1)} collective-permute-done((f32[16,256]{1,0:T(8,128)S(1)}, f32[16,256]{1,0:T(8,128)S(1)}, u32[]{:S(2)}, u32[]{:S(2)}) %collective-permute-start) | collective-permute-done | bytes 16416 | tf_op jit(solution)/shard_map/while/body/eval_jaxpr/ppermute | solution.py:16
  132.5 13.4 %all-to-all-start = ((f32[32,16,256]{2,1,0:T(8,128)}), f32[32,16,256]{2,1,0:T(8,128)S(1)}, u32[]{:S(2)}, u32[]{:S(2)}) async-start(f32[32,16,256]{2,1,0:T(8,128)} %stack.2), calls=%async_computation | async-start | bytes 1048576 | tf_op jit(solution)/shard_map/all_to_all | solution.py:65
  147.6 12.1 %all-to-all-done = f32[32,16,256]{2,1,0:T(8,128)S(1)} async-done(((f32[32,16,256]{2,1,0:T(8,128)}), f32[32,16,256]{2,1,0:T(8,128)S(1)}, u32[]{:S(2)}, u32[]{:S(2)}) %all-to-all-start) | async-done | bytes 524320 | tf_op jit(solution)/shard_map/all_to_all | solution.py:65
  159.7 2.6 copy.18
  162.3 84.0 %gather_fusion = f32[24576,16]{1,0:T(8,128)} fusion(f32[16,8192]{0,1:T(8,128)} %bitcast.89, s32[24576]{0:T(1024)S(1)} %broadcast_clamp_fusion), kind=kCustom, calls=%fused_computation | custom fusion | bytes 3244032 | tf_op jit(solution)/shard_map/jit(_take)/gather | solution.py:69
  246.4 7.6 %copy.20 = f32[24,1024,16]{1,0,2:T(8,128)S(1)} copy(f32[24,1024,16]{2,1,0:T(8,128)} %bitcast.90) | data formatting | bytes 3145728 | tf_op jit(solution)/shard_map/jit(_take)/gather | solution.py:69
  254.0 1.7 fusion
  255.8 8.6 %gather_fusion.1 = f32[2048]{0:T(1024)S(1)} fusion(f32[1024]{0:T(1024)S(1)} %fusion.16, s32[2048]{0:T(1024)S(1)} %broadcast_clamp_fusion.1), kind=kCustom, calls=%fused_computation.1 | custom fusion | bytes 24576 | tf_op jit(solution)/shard_map/jit(_take)/gather | solution.py:74
  265.1 5.6 %all-to-all-start.1 = ((f32[32,1,64]{2,1,0:T(1,128)}), f32[32,1,64]{2,1,0:T(1,128)S(1)}, u32[]{:S(2)}, u32[]{:S(2)}) async-start(f32[32,1,64]{2,1,0:T(1,128)} %and_select_fusion), calls=%async_computation.1 | async-start | bytes 32768 | tf_op jit(solution)/shard_map/all_to_all | solution.py:75
  270.7 10.0 %fusion.23 = f32[128]{0:T(128)S(1)} fusion(f32[]{:T(128)} %bitcast.33, s32[]{:T(128)} %bitcast.34, f32[]{:T(128)} %bitcast.31, s32[]{:T(128)} %bitcast.32, f32[]{:T(128)} %bitcast.29, s32[]{:T(128)} %bitcast.30, f32[]{:T(128)} %bitcast.27, s32[]{:T(128)} %bitcast.28, f32[]{:T(128)} %bitcast.25, s32[]{:T(128)} %bitcast.26, f32[]{:T(128)} %bitcast.23, ...), kind=kLoop, calls=%fused_computation.50 | loop fusion | flops 6144 | bytes 580 | tf_op jit(solution)/shard_map/add | solution.py:97
  283.1 12.7 %scatter_custom_fusion = f32[16385]{0:T(1024)S(1)} fusion(s32[2048]{0:T(1024)S(1)} %bitcast.100, f32[2048]{0:T(1024)S(1)} %reshape.252, f32[]{:T(128)} %constant.61.clone.1), kind=kCustom, calls=%fused_computation.28 | custom fusion | flops 2048 | bytes 65544 | tf_op jit(solution)/shard_map/scatter-add | solution.py:81
  295.8 2.9 collective-permute-start.2
  298.8 5.0 %collective-permute-start.1 = (f32[3,128]{1,0:T(4,128)S(1)}, f32[3,128]{1,0:T(4,128)S(1)}, u32[]{:S(2)}, u32[]{:S(2)}) collective-permute-start(f32[3,128]{1,0:T(4,128)S(1)} %get-tuple-element.40), channel_id=1, source_target_pairs={{0,1},{1,2},{2,3},{3,4},{4,5},{5,6},{6,7},{7,8},{8,9},{9,10},{10,1... | collective-permute-start | bytes 4616 | tf_op jit(solution)/shard_map/ppermute | solution.py:27
  312.5 5.9 %fusion.11 = f32[1,1,128,128]{3,2,1,0:T(8,128)} fusion(f32[1,1,128,128]{3,2,1,0:T(8,128)S(1)} %copy-done.2, f32[134,128]{1,0:T(8,128)S(1)} %pad_maximum_fusion, s32[]{:T(128)S(6)} %select_n.103, s32[]{:T(128)S(6)} %select_n.102, s32[]{:T(128)S(6)} %select_n.101, s32[]{:T(128)S(6)} %select_n.100, s32[]{:T(128)S(6)} %select_n.99, s32[]{:T(128)S(6)} %select_n.98, ...), kind=kLoop, calls=%fused_computation.23 | loop fusion | flops 278528 | bytes 655936 | tf_op jit(solution)/shard_map/broadcast_in_dim | solution.py:99
  (72 shorter events, 36.0 us)
Async XLA Ops:
  0.6 253.4 %copy-start = (f32[24,24]{1,0:T(8,128)S(1)}, f32[24,24]{1,0:T(8,128)}, u32[]{:S(2)}) copy-start(f32[24,24]{1,0:T(8,128)} %param.17) | copy-start | bytes 6916
  1.8 6.3 %collective-permute-start = (f32[16,256]{1,0:T(8,128)S(1)}, f32[16,256]{1,0:T(8,128)S(1)}, u32[]{:S(2)}, u32[]{:S(2)}) collective-permute-start(f32[16,256]{1,0:T(8,128)S(1)} %get-tuple-element.96), channel_id=1, source_target_pairs={{0,32},{32,64},{64,96},{96,128},{128,160},{160,192},{192,224},{224... | collective-permute-start | bytes 49160 | tf_op jit(solution)/shard_map/while/body/eval_jaxpr/ppermute | solution.py:16
  10.5 6.3 %collective-permute-start = (f32[16,256]{1,0:T(8,128)S(1)}, f32[16,256]{1,0:T(8,128)S(1)}, u32[]{:S(2)}, u32[]{:S(2)}) collective-permute-start(f32[16,256]{1,0:T(8,128)S(1)} %get-tuple-element.96), channel_id=1, source_target_pairs={{0,32},{32,64},{64,96},{96,128},{128,160},{160,192},{192,224},{224... | collective-permute-start | bytes 49160 | tf_op jit(solution)/shard_map/while/body/eval_jaxpr/ppermute | solution.py:16
  19.1 6.3 %collective-permute-start = (f32[16,256]{1,0:T(8,128)S(1)}, f32[16,256]{1,0:T(8,128)S(1)}, u32[]{:S(2)}, u32[]{:S(2)}) collective-permute-start(f32[16,256]{1,0:T(8,128)S(1)} %get-tuple-element.96), channel_id=1, source_target_pairs={{0,32},{32,64},{64,96},{96,128},{128,160},{160,192},{192,224},{224... | collective-permute-start | bytes 49160 | tf_op jit(solution)/shard_map/while/body/eval_jaxpr/ppermute | solution.py:16
  27.8 6.3 %collective-permute-start = (f32[16,256]{1,0:T(8,128)S(1)}, f32[16,256]{1,0:T(8,128)S(1)}, u32[]{:S(2)}, u32[]{:S(2)}) collective-permute-start(f32[16,256]{1,0:T(8,128)S(1)} %get-tuple-element.96), channel_id=1, source_target_pairs={{0,32},{32,64},{64,96},{96,128},{128,160},{160,192},{192,224},{224... | collective-permute-start | bytes 49160 | tf_op jit(solution)/shard_map/while/body/eval_jaxpr/ppermute | solution.py:16
  36.4 6.3 %collective-permute-start = (f32[16,256]{1,0:T(8,128)S(1)}, f32[16,256]{1,0:T(8,128)S(1)}, u32[]{:S(2)}, u32[]{:S(2)}) collective-permute-start(f32[16,256]{1,0:T(8,128)S(1)} %get-tuple-element.96), channel_id=1, source_target_pairs={{0,32},{32,64},{64,96},{96,128},{128,160},{160,192},{192,224},{224... | collective-permute-start | bytes 49160 | tf_op jit(solution)/shard_map/while/body/eval_jaxpr/ppermute | solution.py:16
  45.1 6.3 %collective-permute-start = (f32[16,256]{1,0:T(8,128)S(1)}, f32[16,256]{1,0:T(8,128)S(1)}, u32[]{:S(2)}, u32[]{:S(2)}) collective-permute-start(f32[16,256]{1,0:T(8,128)S(1)} %get-tuple-element.96), channel_id=1, source_target_pairs={{0,32},{32,64},{64,96},{96,128},{128,160},{160,192},{192,224},{224... | collective-permute-start | bytes 49160 | tf_op jit(solution)/shard_map/while/body/eval_jaxpr/ppermute | solution.py:16
  53.7 6.3 %collective-permute-start = (f32[16,256]{1,0:T(8,128)S(1)}, f32[16,256]{1,0:T(8,128)S(1)}, u32[]{:S(2)}, u32[]{:S(2)}) collective-permute-start(f32[16,256]{1,0:T(8,128)S(1)} %get-tuple-element.96), channel_id=1, source_target_pairs={{0,32},{32,64},{64,96},{96,128},{128,160},{160,192},{192,224},{224... | collective-permute-start | bytes 49160 | tf_op jit(solution)/shard_map/while/body/eval_jaxpr/ppermute | solution.py:16
  62.4 6.3 %collective-permute-start = (f32[16,256]{1,0:T(8,128)S(1)}, f32[16,256]{1,0:T(8,128)S(1)}, u32[]{:S(2)}, u32[]{:S(2)}) collective-permute-start(f32[16,256]{1,0:T(8,128)S(1)} %get-tuple-element.96), channel_id=1, source_target_pairs={{0,32},{32,64},{64,96},{96,128},{128,160},{160,192},{192,224},{224... | collective-permute-start | bytes 49160 | tf_op jit(solution)/shard_map/while/body/eval_jaxpr/ppermute | solution.py:16
  71.0 6.3 %collective-permute-start = (f32[16,256]{1,0:T(8,128)S(1)}, f32[16,256]{1,0:T(8,128)S(1)}, u32[]{:S(2)}, u32[]{:S(2)}) collective-permute-start(f32[16,256]{1,0:T(8,128)S(1)} %get-tuple-element.96), channel_id=1, source_target_pairs={{0,32},{32,64},{64,96},{96,128},{128,160},{160,192},{192,224},{224... | collective-permute-start | bytes 49160 | tf_op jit(solution)/shard_map/while/body/eval_jaxpr/ppermute | solution.py:16
  79.7 6.3 %collective-permute-start = (f32[16,256]{1,0:T(8,128)S(1)}, f32[16,256]{1,0:T(8,128)S(1)}, u32[]{:S(2)}, u32[]{:S(2)}) collective-permute-start(f32[16,256]{1,0:T(8,128)S(1)} %get-tuple-element.96), channel_id=1, source_target_pairs={{0,32},{32,64},{64,96},{96,128},{128,160},{160,192},{192,224},{224... | collective-permute-start | bytes 49160 | tf_op jit(solution)/shard_map/while/body/eval_jaxpr/ppermute | solution.py:16
  88.3 6.3 %collective-permute-start = (f32[16,256]{1,0:T(8,128)S(1)}, f32[16,256]{1,0:T(8,128)S(1)}, u32[]{:S(2)}, u32[]{:S(2)}) collective-permute-start(f32[16,256]{1,0:T(8,128)S(1)} %get-tuple-element.96), channel_id=1, source_target_pairs={{0,32},{32,64},{64,96},{96,128},{128,160},{160,192},{192,224},{224... | collective-permute-start | bytes 49160 | tf_op jit(solution)/shard_map/while/body/eval_jaxpr/ppermute | solution.py:16
  97.0 6.3 %collective-permute-start = (f32[16,256]{1,0:T(8,128)S(1)}, f32[16,256]{1,0:T(8,128)S(1)}, u32[]{:S(2)}, u32[]{:S(2)}) collective-permute-start(f32[16,256]{1,0:T(8,128)S(1)} %get-tuple-element.96), channel_id=1, source_target_pairs={{0,32},{32,64},{64,96},{96,128},{128,160},{160,192},{192,224},{224... | collective-permute-start | bytes 49160 | tf_op jit(solution)/shard_map/while/body/eval_jaxpr/ppermute | solution.py:16
  105.6 6.3 %collective-permute-start = (f32[16,256]{1,0:T(8,128)S(1)}, f32[16,256]{1,0:T(8,128)S(1)}, u32[]{:S(2)}, u32[]{:S(2)}) collective-permute-start(f32[16,256]{1,0:T(8,128)S(1)} %get-tuple-element.96), channel_id=1, source_target_pairs={{0,32},{32,64},{64,96},{96,128},{128,160},{160,192},{192,224},{224... | collective-permute-start | bytes 49160 | tf_op jit(solution)/shard_map/while/body/eval_jaxpr/ppermute | solution.py:16
  114.3 6.3 %collective-permute-start = (f32[16,256]{1,0:T(8,128)S(1)}, f32[16,256]{1,0:T(8,128)S(1)}, u32[]{:S(2)}, u32[]{:S(2)}) collective-permute-start(f32[16,256]{1,0:T(8,128)S(1)} %get-tuple-element.96), channel_id=1, source_target_pairs={{0,32},{32,64},{64,96},{96,128},{128,160},{160,192},{192,224},{224... | collective-permute-start | bytes 49160 | tf_op jit(solution)/shard_map/while/body/eval_jaxpr/ppermute | solution.py:16
  122.9 6.3 %collective-permute-start = (f32[16,256]{1,0:T(8,128)S(1)}, f32[16,256]{1,0:T(8,128)S(1)}, u32[]{:S(2)}, u32[]{:S(2)}) collective-permute-start(f32[16,256]{1,0:T(8,128)S(1)} %get-tuple-element.96), channel_id=1, source_target_pairs={{0,32},{32,64},{64,96},{96,128},{128,160},{160,192},{192,224},{224... | collective-permute-start | bytes 49160 | tf_op jit(solution)/shard_map/while/body/eval_jaxpr/ppermute | solution.py:16
  131.6 30.8 %copy-start.3 = (f32[16,256]{1,0:T(8,128)}, f32[16,256]{1,0:T(8,128)S(1)}, u32[]{:S(2)}) copy-start(f32[16,256]{1,0:T(8,128)S(1)} %get-tuple-element.29) | copy-start | bytes 49156
  131.6 14.4 %copy-start.9 = (s32[1,1,1024]{2,1,0:T(1,128)S(1)}, s32[1,1,1024]{2,1,0:T(1,128)}, u32[]{:S(2)}) copy-start(s32[1,1,1024]{2,1,0:T(1,128)} %param.18) | copy-start | bytes 12292
  131.6 14.4 %copy-start.1 = (s32[1,1,24,1024]{3,2,1,0:T(8,128)S(1)}, s32[1,1,24,1024]{3,2,1,0:T(8,128)}, u32[]{:S(2)}) copy-start(s32[1,1,24,1024]{3,2,1,0:T(8,128)} %param.19) | copy-start | bytes 294916
  131.6 14.4 %copy-start.7 = (s32[1,1,32,64]{3,2,1,0:T(8,128)S(1)}, s32[1,1,32,64]{3,2,1,0:T(8,128)}, u32[]{:S(2)}) copy-start(s32[1,1,32,64]{3,2,1,0:T(8,128)} %param.22) | copy-start | bytes 24580
  131.6 14.5 %copy-start.4 = (s32[1,1,32,64]{3,2,1,0:T(8,128)S(1)}, s32[1,1,32,64]{3,2,1,0:T(8,128)}, u32[]{:S(2)}) copy-start(s32[1,1,32,64]{3,2,1,0:T(8,128)} %param.21) | copy-start | bytes 24580
  131.6 14.6 %copy-start.5 = (s32[8]{0:T(128)S(1)}, s32[8]{0:T(128)}, u32[]{:S(2)}) copy-start(s32[8]{0:T(128)} %param.24) | copy-start | bytes 100
  131.6 15.3 %copy-start.6 = (f32[8]{0:T(128)S(1)}, f32[8]{0:T(128)}, u32[]{:S(2)}) copy-start(f32[8]{0:T(128)} %param.25) | copy-start | bytes 100
  132.5 27.2 %all-to-all-start = ((f32[32,16,256]{2,1,0:T(8,128)}), f32[32,16,256]{2,1,0:T(8,128)S(1)}, u32[]{:S(2)}, u32[]{:S(2)}) async-start(f32[32,16,256]{2,1,0:T(8,128)} %stack.2), calls=%async_computation | async-start | bytes 1048576 | tf_op jit(solution)/shard_map/all_to_all | solution.py:65
  254.0 1.7 copy-start.8
  255.8 40.1 %copy-start.2 = (f32[1,1,128,128]{3,2,1,0:T(8,128)S(1)}, f32[1,1,128,128]{3,2,1,0:T(8,128)}, u32[]{:S(2)}) copy-start(f32[1,1,128,128]{3,2,1,0:T(8,128)} %param.23) | copy-start | bytes 196612
  265.1 16.7 %all-to-all-start.1 = ((f32[32,1,64]{2,1,0:T(1,128)}), f32[32,1,64]{2,1,0:T(1,128)S(1)}, u32[]{:S(2)}, u32[]{:S(2)}) async-start(f32[32,1,64]{2,1,0:T(1,128)} %and_select_fusion), calls=%async_computation.1 | async-start | bytes 32768 | tf_op jit(solution)/shard_map/all_to_all | solution.py:75
  295.8 16.6 %collective-permute-start.2 = (f32[3,128]{1,0:T(4,128)S(1)}, f32[3,128]{1,0:T(4,128)S(1)}, u32[]{:S(2)}, u32[]{:S(2)}) collective-permute-start(f32[3,128]{1,0:T(4,128)S(1)} %get-tuple-element.41), channel_id=1, source_target_pairs={{1,0},{2,1},{3,2},{4,3},{5,4},{6,5},{7,6},{8,7},{9,8},{10,9},{11,1... | collective-permute-start | bytes 4616 | tf_op jit(solution)/shard_map/ppermute | solution.py:29
  298.8 13.7 %collective-permute-start.1 = (f32[3,128]{1,0:T(4,128)S(1)}, f32[3,128]{1,0:T(4,128)S(1)}, u32[]{:S(2)}, u32[]{:S(2)}) collective-permute-start(f32[3,128]{1,0:T(4,128)S(1)} %get-tuple-element.40), channel_id=1, source_target_pairs={{0,1},{1,2},{2,3},{3,4},{4,5},{5,6},{6,7},{7,8},{8,9},{9,10},{10,1... | collective-permute-start | bytes 4616 | tf_op jit(solution)/shard_map/ppermute | solution.py:27
